TPU v7x, 32 devices: a whole 2x2x4 slice. The times are simulated.
32 devices in a mesh: tm: 8 (over y, x, core), space: 4 (over z).
Axes of the slice: x: 2, y: 2, z: 4, core: 2. Of those that a mesh axis runs over, the one named last changes fastest.
Arguments:
- starts: float32 [8, 32, 128, 128], P('tm', 'space'), may hold values from -6 to 6
- diffusivity: float32 [32, 128, 128], P('space'), may hold values from 0.04 to 0.2
- velocity: float32 [2, 32, 128, 128], P(None, 'space'), may hold values from -0.1 to 0.1
- obstacle: int32 [32, 128, 128], P('space'), may hold values from 0 to 1, as said below
- substep_scale: float32 [12], replicated, may hold values from 0.5 to 1
- neighbors: int32 [32, 4], P('space'), may hold values from 0 to 32, as said below
- coarse_x: float32 [32, 64, 64], P('space'), may hold values from -1 to 1
- coarse_y: float32 [32, 128, 128], P('space'), may hold values from -1 to 1
Outputs:
- slice_ends: float32 [8, 32, 128, 128], P('tm', 'space')
- increment: float32 [8, 32, 128, 128], P('tm', 'space')
Inputs may be any that keep to these rules, and one draw needn't show every extreme that they name: `neighbors`: tiles form a grid of 4 by 8; each entry names the tile beside a tile in the given direction, or 32 on the grid's edge. The tiles 8 * k to 8 * (k + 1) - 1 fill grid row k, in any order within it, so a neighbour's number differs from the tile's block k by at most one block. `obstacle`: each tile holds one tube, a disc of radius 128 // 8 to 32 cells.
All inputs are finite; a program needn't handle non-finite values.
Results may differ from a plain program's by a relative error of at most 0.0002.
Values sent between devices are 32-bit elements; how exact they have to be, the bound alone decides.
No kernel may reach another device: no remote copies, remote signals or barrier semaphores. Data moves between devices by JAX's collectives and lax.ppermute only.
A program may use at most 128 MiB of HBM per device.

v0:
```python
import jax
import jax.numpy as jnp
from jax import lax
from jax.sharding import PartitionSpec as P

SUB = 12
exact_precision = lax.Precision.HIGHEST


def padded(block, sides, width):
    for axis, dim in sides:
        count = lax.axis_size(axis)
        forward = [(i, i + 1) for i in range(count - 1)]
        backward = [(target, source) for source, target in forward]
        low = lax.ppermute(
            lax.slice_in_dim(block, block.shape[dim] - width, None, axis=dim), axis, forward
        )
        high = lax.ppermute(lax.slice_in_dim(block, 0, width, axis=dim), axis, backward)
        block = jnp.concatenate([low, block, high], axis=dim)
    return block


def spread(value, axis, source):
    kept = jnp.where(lax.axis_index(axis) == source, value, 0).astype(value.dtype)
    return lax.psum(kept, axis)


def passed_along(block, axis, distance):
    devices = range(lax.axis_size(axis))
    route = [(i - distance, i) for i in devices if i - distance in devices]
    return lax.ppermute(block, axis, route)


def restrict(values):
    return 0.5 * (values[..., 0::2, :] + values[..., 1::2, :])


def prolong(coarse_values):
    return jnp.repeat(coarse_values, 2, axis=-2)


def apply_coarse(coarse_values, matrix_x, matrix_y):
    mixed_x = jnp.einsum("tij,...tjk->...tik", matrix_x, coarse_values, precision=exact_precision)
    return jnp.einsum("...tik,tlk->...til", mixed_x, matrix_y, precision=exact_precision)


def on_device(
    starts, diffusivity, velocity, obstacle, substep_scale, neighbors, coarse_x, coarse_y
):
    slice_count = starts.shape[0]
    tile_count = starts.shape[1]
    all_tiles = tile_count * lax.axis_size("space")
    block_base = lax.axis_index("space") * tile_count
    open_cells = 1.0 - obstacle.astype(jnp.float32)
    speed_x = velocity[0]
    speed_y = velocity[1]
    shifted = neighbors - block_base + tile_count
    lookup_index = jnp.where(neighbors == all_tiles, 3 * tile_count, shifted)

    def advance(substep_index, current):
        strength = substep_scale[substep_index]
        own_faces = jnp.stack(
            [current[:, :, 0, :], current[:, :, -1, :], current[:, :, :, 0], current[:, :, :, -1]],
            axis=2,
        )
        gathered = padded(own_faces, (("space", 1),), tile_count)
        gathered = jnp.concatenate([gathered, jnp.zeros_like(gathered[:, :1])], axis=1)
        west_face = gathered[:, lookup_index[:, 0], 1]
        east_face = gathered[:, lookup_index[:, 1], 0]
        south_face = gathered[:, lookup_index[:, 2], 3]
        north_face = gathered[:, lookup_index[:, 3], 2]
        from_west = jnp.concatenate([west_face[:, :, None, :], current[:, :, :-1, :]], axis=2)
        from_east = jnp.concatenate([current[:, :, 1:, :], east_face[:, :, None, :]], axis=2)
        from_south = jnp.concatenate([south_face[:, :, :, None], current[:, :, :, :-1]], axis=3)
        from_north = jnp.concatenate([current[:, :, :, 1:], north_face[:, :, :, None]], axis=3)
        laplace = from_west + from_east + from_south + from_north - 4.0 * current
        transport = speed_x * (from_east - from_west) + speed_y * (from_north - from_south)
        return open_cells * (current + strength * diffusivity * laplace - 0.5 * transport)

    fine_ends = lax.fori_loop(0, SUB, advance, starts)
    correction = fine_ends - prolong(apply_coarse(restrict(starts), coarse_x, coarse_y))
    coarse_jump = restrict(correction)
    first_coarse = spread(restrict(starts[0]), "tm", 0)
    every_jump = lax.all_gather(coarse_jump, "tm", axis=0, tiled=True)

    def sweep(state_now, jump):
        return (apply_coarse(state_now, coarse_x, coarse_y) + jump, state_now)

    last_state, history = lax.scan(sweep, first_coarse, every_jump)
    own_coarse = lax.dynamic_slice_in_dim(
        history, lax.axis_index("tm") * slice_count, slice_count, 0
    )
    slice_ends = prolong(apply_coarse(own_coarse, coarse_x, coarse_y)) + correction
    previous = passed_along(slice_ends[-1], "tm", 1)
    first_step = jnp.where(
        lax.axis_index("tm") == 0, jnp.zeros_like(previous), previous - starts[0]
    )
    increment = jnp.concatenate([first_step[None], slice_ends[:-1] - starts[1:]], axis=0)
    return (slice_ends, increment)


def solution(mesh):
    placed = (
        P("tm", "space", None, None),
        P("space", None, None),
        P(None, "space", None, None),
        P("space", None, None),
        P(),
        P("space", None),
        P("space", None, None),
        P("space", None, None),
    )
    return jax.shard_map(
        on_device,
        mesh=mesh,
        in_specs=placed,
        out_specs=(P("tm", "space", None, None), P("tm", "space", None, None)),
        check_vma=False,
    )
```

profile of v0, /device:TPU:4, one launch (start us, length us, event | category | flops | bytes accessed | tf_op | source)
XLA Modules:
  0.0 285.6 jit_solution(6165159158150083791)
XLA Ops:
  16.3 170.8 %while.25 = (s32[]{:T(128)}, f32[1,8,128,128]{2,1,3,0:T(8,128)S(1)}, f32[8,128,128]{1,0,2:T(8,128)}, f32[12]{0:T(128)S(1)}, f32[8,128,128]{1,0,2:T(8,128)}, /*in...) while((s32[]{:T(128)}, ...), condition=%wide.region_2.3_spmd, body=%wide.region_1.2_spmd.sunk | while | flops 2710714 | bytes 10800037 | solution.py:80
  16.6 3.5 %collective-permute-start.1 = (f32[1,8,4,128]{3,2,1,0:T(4,128)S(1)}, f32[1,8,4,128]{3,2,1,0:T(4,128)S(1)}, u32[]{:S(2)}, u32[]{:S(2)}) collective-permute-start(f32[1,8,4,128]{3,2,1,0:T(4,128)S(1)} %pad_maximum_fusion.6), channel_id=1, source_target_pairs={{0,1},{1,2},{2,3},{4,5},{5,6},{6,7},{8,9},{9,10},{10,11},{12,13},{... | collective-permute-start | bytes 49160 | tf_op jit(solution)/shard_map/while/body/eval_jaxpr/ppermute | solution.py:15
  23.1 2.6 collective-permute-done
  28.7 3.0 %fusion.60 = f32[1,8,128,128]{2,1,3,0:T(8,128)S(1)} fusion(f32[1,8,128,128]{2,1,3,0:T(8,128)S(1)} %get-tuple-element.355, f32[8,128,128]{1,0,2:T(8,128)} %get-tuple-element.367, f32[1,8,128,128]{2,1,3,0:T(8,128)} %get-tuple-element.372, f32[1,8,128,128]{2,1,3,0:T(8,128)} %get-tuple-element.371, f32[1,8,128,1]{2,1,3,0:T(8,128)S(1)} %bitcast.113, ...), kind=kLoop, calls=%fused_computation.13.clone.1 | loop fusion | flops 2621440 | bytes 5242884 | tf_op jit(solution)/shard_map/while/body/eval_jaxpr/mul | solution.py:78
  31.9 3.5 %collective-permute-start.1 = (f32[1,8,4,128]{3,2,1,0:T(4,128)S(1)}, f32[1,8,4,128]{3,2,1,0:T(4,128)S(1)}, u32[]{:S(2)}, u32[]{:S(2)}) collective-permute-start(f32[1,8,4,128]{3,2,1,0:T(4,128)S(1)} %pad_maximum_fusion.6), channel_id=1, source_target_pairs={{0,1},{1,2},{2,3},{4,5},{5,6},{6,7},{8,9},{9,10},{10,11},{12,13},{... | collective-permute-start | bytes 49160 | tf_op jit(solution)/shard_map/while/body/eval_jaxpr/ppermute | solution.py:15
  38.5 2.6 collective-permute-done
  44.0 3.0 %fusion.60 = f32[1,8,128,128]{2,1,3,0:T(8,128)S(1)} fusion(f32[1,8,128,128]{2,1,3,0:T(8,128)S(1)} %get-tuple-element.355, f32[8,128,128]{1,0,2:T(8,128)} %get-tuple-element.367, f32[1,8,128,128]{2,1,3,0:T(8,128)} %get-tuple-element.372, f32[1,8,128,128]{2,1,3,0:T(8,128)} %get-tuple-element.371, f32[1,8,128,1]{2,1,3,0:T(8,128)S(1)} %bitcast.113, ...), kind=kLoop, calls=%fused_computation.13.clone.1 | loop fusion | flops 2621440 | bytes 5242884 | tf_op jit(solution)/shard_map/while/body/eval_jaxpr/mul | solution.py:78
  47.3 3.5 %collective-permute-start.1 = (f32[1,8,4,128]{3,2,1,0:T(4,128)S(1)}, f32[1,8,4,128]{3,2,1,0:T(4,128)S(1)}, u32[]{:S(2)}, u32[]{:S(2)}) collective-permute-start(f32[1,8,4,128]{3,2,1,0:T(4,128)S(1)} %pad_maximum_fusion.6), channel_id=1, source_target_pairs={{0,1},{1,2},{2,3},{4,5},{5,6},{6,7},{8,9},{9,10},{10,11},{12,13},{... | collective-permute-start | bytes 49160 | tf_op jit(solution)/shard_map/while/body/eval_jaxpr/ppermute | solution.py:15
  53.9 2.6 collective-permute-done
  59.4 3.0 %fusion.60 = f32[1,8,128,128]{2,1,3,0:T(8,128)S(1)} fusion(f32[1,8,128,128]{2,1,3,0:T(8,128)S(1)} %get-tuple-element.355, f32[8,128,128]{1,0,2:T(8,128)} %get-tuple-element.367, f32[1,8,128,128]{2,1,3,0:T(8,128)} %get-tuple-element.372, f32[1,8,128,128]{2,1,3,0:T(8,128)} %get-tuple-element.371, f32[1,8,128,1]{2,1,3,0:T(8,128)S(1)} %bitcast.113, ...), kind=kLoop, calls=%fused_computation.13.clone.1 | loop fusion | flops 2621440 | bytes 5242884 | tf_op jit(solution)/shard_map/while/body/eval_jaxpr/mul | solution.py:78
  62.7 2.0 collective-permute-start.1
  67.7 2.6 collective-permute-done
  73.3 3.0 %fusion.60 = f32[1,8,128,128]{2,1,3,0:T(8,128)S(1)} fusion(f32[1,8,128,128]{2,1,3,0:T(8,128)S(1)} %get-tuple-element.355, f32[8,128,128]{1,0,2:T(8,128)} %get-tuple-element.367, f32[1,8,128,128]{2,1,3,0:T(8,128)} %get-tuple-element.372, f32[1,8,128,128]{2,1,3,0:T(8,128)} %get-tuple-element.371, f32[1,8,128,1]{2,1,3,0:T(8,128)S(1)} %bitcast.113, ...), kind=kLoop, calls=%fused_computation.13.clone.1 | loop fusion | flops 2621440 | bytes 5242884 | tf_op jit(solution)/shard_map/while/body/eval_jaxpr/mul | solution.py:78
  81.6 2.6 collective-permute-done
  87.1 3.0 %fusion.60 = f32[1,8,128,128]{2,1,3,0:T(8,128)S(1)} fusion(f32[1,8,128,128]{2,1,3,0:T(8,128)S(1)} %get-tuple-element.355, f32[8,128,128]{1,0,2:T(8,128)} %get-tuple-element.367, f32[1,8,128,128]{2,1,3,0:T(8,128)} %get-tuple-element.372, f32[1,8,128,128]{2,1,3,0:T(8,128)} %get-tuple-element.371, f32[1,8,128,1]{2,1,3,0:T(8,128)S(1)} %bitcast.113, ...), kind=kLoop, calls=%fused_computation.13.clone.1 | loop fusion | flops 2621440 | bytes 5242884 | tf_op jit(solution)/shard_map/while/body/eval_jaxpr/mul | solution.py:78
  90.4 2.0 collective-permute-start.1
  95.5 2.6 collective-permute-done
  101.0 3.0 %fusion.60 = f32[1,8,128,128]{2,1,3,0:T(8,128)S(1)} fusion(f32[1,8,128,128]{2,1,3,0:T(8,128)S(1)} %get-tuple-element.355, f32[8,128,128]{1,0,2:T(8,128)} %get-tuple-element.367, f32[1,8,128,128]{2,1,3,0:T(8,128)} %get-tuple-element.372, f32[1,8,128,128]{2,1,3,0:T(8,128)} %get-tuple-element.371, f32[1,8,128,1]{2,1,3,0:T(8,128)S(1)} %bitcast.113, ...), kind=kLoop, calls=%fused_computation.13.clone.1 | loop fusion | flops 2621440 | bytes 5242884 | tf_op jit(solution)/shard_map/while/body/eval_jaxpr/mul | solution.py:78
  104.3 2.0 collective-permute-start.1
  109.3 2.6 collective-permute-done
  114.9 3.0 %fusion.60 = f32[1,8,128,128]{2,1,3,0:T(8,128)S(1)} fusion(f32[1,8,128,128]{2,1,3,0:T(8,128)S(1)} %get-tuple-element.355, f32[8,128,128]{1,0,2:T(8,128)} %get-tuple-element.367, f32[1,8,128,128]{2,1,3,0:T(8,128)} %get-tuple-element.372, f32[1,8,128,128]{2,1,3,0:T(8,128)} %get-tuple-element.371, f32[1,8,128,1]{2,1,3,0:T(8,128)S(1)} %bitcast.113, ...), kind=kLoop, calls=%fused_computation.13.clone.1 | loop fusion | flops 2621440 | bytes 5242884 | tf_op jit(solution)/shard_map/while/body/eval_jaxpr/mul | solution.py:78
  118.1 2.0 collective-permute-start.1
  123.2 2.6 collective-permute-done
  128.7 3.0 %fusion.60 = f32[1,8,128,128]{2,1,3,0:T(8,128)S(1)} fusion(f32[1,8,128,128]{2,1,3,0:T(8,128)S(1)} %get-tuple-element.355, f32[8,128,128]{1,0,2:T(8,128)} %get-tuple-element.367, f32[1,8,128,128]{2,1,3,0:T(8,128)} %get-tuple-element.372, f32[1,8,128,128]{2,1,3,0:T(8,128)} %get-tuple-element.371, f32[1,8,128,1]{2,1,3,0:T(8,128)S(1)} %bitcast.113, ...), kind=kLoop, calls=%fused_computation.13.clone.1 | loop fusion | flops 2621440 | bytes 5242884 | tf_op jit(solution)/shard_map/while/body/eval_jaxpr/mul | solution.py:78
  132.0 2.0 collective-permute-start.1
  137.0 2.6 collective-permute-done
  142.6 3.0 %fusion.60 = f32[1,8,128,128]{2,1,3,0:T(8,128)S(1)} fusion(f32[1,8,128,128]{2,1,3,0:T(8,128)S(1)} %get-tuple-element.355, f32[8,128,128]{1,0,2:T(8,128)} %get-tuple-element.367, f32[1,8,128,128]{2,1,3,0:T(8,128)} %get-tuple-element.372, f32[1,8,128,128]{2,1,3,0:T(8,128)} %get-tuple-element.371, f32[1,8,128,1]{2,1,3,0:T(8,128)S(1)} %bitcast.113, ...), kind=kLoop, calls=%fused_computation.13.clone.1 | loop fusion | flops 2621440 | bytes 5242884 | tf_op jit(solution)/shard_map/while/body/eval_jaxpr/mul | solution.py:78
  145.8 2.0 collective-permute-start.1
  150.9 2.6 collective-permute-done
  156.4 3.0 %fusion.60 = f32[1,8,128,128]{2,1,3,0:T(8,128)S(1)} fusion(f32[1,8,128,128]{2,1,3,0:T(8,128)S(1)} %get-tuple-element.355, f32[8,128,128]{1,0,2:T(8,128)} %get-tuple-element.367, f32[1,8,128,128]{2,1,3,0:T(8,128)} %get-tuple-element.372, f32[1,8,128,128]{2,1,3,0:T(8,128)} %get-tuple-element.371, f32[1,8,128,1]{2,1,3,0:T(8,128)S(1)} %bitcast.113, ...), kind=kLoop, calls=%fused_computation.13.clone.1 | loop fusion | flops 2621440 | bytes 5242884 | tf_op jit(solution)/shard_map/while/body/eval_jaxpr/mul | solution.py:78
  159.7 2.0 collective-permute-start.1
  164.8 2.6 collective-permute-done
  170.3 3.0 %fusion.60 = f32[1,8,128,128]{2,1,3,0:T(8,128)S(1)} fusion(f32[1,8,128,128]{2,1,3,0:T(8,128)S(1)} %get-tuple-element.355, f32[8,128,128]{1,0,2:T(8,128)} %get-tuple-element.367, f32[1,8,128,128]{2,1,3,0:T(8,128)} %get-tuple-element.372, f32[1,8,128,128]{2,1,3,0:T(8,128)} %get-tuple-element.371, f32[1,8,128,1]{2,1,3,0:T(8,128)S(1)} %bitcast.113, ...), kind=kLoop, calls=%fused_computation.13.clone.1 | loop fusion | flops 2621440 | bytes 5242884 | tf_op jit(solution)/shard_map/while/body/eval_jaxpr/mul | solution.py:78
  173.6 2.0 collective-permute-start.1
  178.6 2.6 collective-permute-done
  184.2 3.0 %fusion.60 = f32[1,8,128,128]{2,1,3,0:T(8,128)S(1)} fusion(f32[1,8,128,128]{2,1,3,0:T(8,128)S(1)} %get-tuple-element.355, f32[8,128,128]{1,0,2:T(8,128)} %get-tuple-element.367, f32[1,8,128,128]{2,1,3,0:T(8,128)} %get-tuple-element.372, f32[1,8,128,128]{2,1,3,0:T(8,128)} %get-tuple-element.371, f32[1,8,128,1]{2,1,3,0:T(8,128)S(1)} %bitcast.113, ...), kind=kLoop, calls=%fused_computation.13.clone.1 | loop fusion | flops 2621440 | bytes 5242884 | tf_op jit(solution)/shard_map/while/body/eval_jaxpr/mul | solution.py:78
  191.3 26.0 %all-gather.2.cloned.1.call-done = f32[8,8,64,128]{3,2,1,0:T(8,128)} async-done(((f32[1,8,64,128]{3,2,1,0:T(8,128)}), f32[8,8,64,128]{3,2,1,0:T(8,128)}) %all-gather.2.cloned.1.call-update) | async-done | bytes 2097168 | tf_op jit(solution)/shard_map/all_gather | solution.py:84
  217.2 46.5 %while.26 = (s32[]{:T(128)}, f32[8,64,128]{2,1,0:T(8,128)}, f32[8,8,64,128]{3,2,1,0:T(8,128)}, f32[8,64,64]{2,1,0:T(8,128)S(1)}, f32[8,128,128]{2,1,0:T(8,128)S(1)}, /*index=5*/f32[8,8,64,128]{3,2,1,0:T(8,128)}, s32[]{:T(128)}) while((s32[]{:T(128)}, f32[8,64,128]{2,1,0:T(8,128)}, f32[8,8,64,128]{3,2,1,0:T(8,128)}, ...), condition=%wide.region_4.5_spmd, body=%wide.region_3.4_spmd.sunk | while | flops 151060480 | bytes 2490461 | solution.py:89
  220.3 2.8 convolution_add_fusion.2
  226.1 2.8 convolution_add_fusion.2
  231.9 2.8 convolution_add_fusion.2
  237.7 2.8 convolution_add_fusion.2
  243.5 2.8 convolution_add_fusion.2
  249.3 2.8 convolution_add_fusion.2
  255.1 2.8 convolution_add_fusion.2
  260.9 2.8 convolution_add_fusion.2
  266.5 2.1 collective-permute-start.2
  268.6 9.3 %collective-permute-done.2 = f32[8,128,128]{2,1,0:T(8,128)S(1)} collective-permute-done((f32[8,128,128]{2,1,0:T(8,128)S(1)}, f32[8,128,128]{2,1,0:T(8,128)S(1)}, u32[]{:S(2)}, u32[]{:S(2)}) %collective-permute-start.2) | collective-permute-done | bytes 524320 | tf_op jit(solution)/shard_map/ppermute | solution.py:31
  (285 shorter events, 117.6 us)
Async XLA Ops:
  7.2 3.1 %copy-start.2 = (f32[1,8,128,128]{3,2,1,0:T(8,128)S(1)}, f32[1,8,128,128]{3,2,1,0:T(8,128)}, u32[]{:S(2)}) copy-start(f32[1,8,128,128]{3,2,1,0:T(8,128)} %param.12) | copy-start | bytes 1572868
  7.2 184.1 %all-reduce.6.cloned.1.call-start = ((), (), s32[]{:S(2)}) async-start(), calls=%async_computation | async-start | bytes 524288 | tf_op jit(solution)/shard_map/psum | solution.py:25
  7.2 4.8 %copy-start.6 = (f32[8,128,128]{2,1,0:T(8,128)S(1)}, f32[8,128,128]{2,1,0:T(8,128)}, u32[]{:S(2)}) copy-start(f32[8,128,128]{2,1,0:T(8,128)} %param.13) | copy-start | bytes 1572868
  9.4 3.6 %copy-start.7 = (s32[8,128,128]{2,1,0:T(8,128)S(1)}, s32[8,128,128]{2,1,0:T(8,128)}, u32[]{:S(2)}) copy-start(s32[8,128,128]{2,1,0:T(8,128)} %param.15) | copy-start | bytes 1572868
  10.2 207.0 %all-gather.2.cloned.1.call-start = ((), (), s32[]{:S(2)}) async-start(), calls=%async_computation.1 | async-start | bytes 2359296 | tf_op jit(solution)/shard_map/all_gather | solution.py:84
  11.8 2.3 copy-start.4
  14.1 2.1 copy-start.8
  14.1 2.1 copy-start.9
  16.3 171.1 %copy-start.1 = (f32[8,64,64]{2,1,0:T(8,128)S(1)}, f32[8,64,64]{2,1,0:T(8,128)}, u32[]{:S(2)}) copy-start(f32[8,64,64]{2,1,0:T(8,128)} %param.18) | copy-start | bytes 393220
  16.6 6.6 %collective-permute-start.1 = (f32[1,8,4,128]{3,2,1,0:T(4,128)S(1)}, f32[1,8,4,128]{3,2,1,0:T(4,128)S(1)}, u32[]{:S(2)}, u32[]{:S(2)}) collective-permute-start(f32[1,8,4,128]{3,2,1,0:T(4,128)S(1)} %pad_maximum_fusion.6), channel_id=1, source_target_pairs={{0,1},{1,2},{2,3},{4,5},{5,6},{6,7},{8,9},{9,10},{10,11},{12,13},{... | collective-permute-start | bytes 49160 | tf_op jit(solution)/shard_map/while/body/eval_jaxpr/ppermute | solution.py:15
  20.1 5.6 %collective-permute-start = (f32[1,8,4,128]{3,2,1,0:T(4,128)S(1)}, f32[1,8,4,128]{3,2,1,0:T(4,128)S(1)}, u32[]{:S(2)}, u32[]{:S(2)}) collective-permute-start(f32[1,8,4,128]{3,2,1,0:T(4,128)S(1)} %pad_maximum_fusion.6), channel_id=1, source_target_pairs={{1,0},{2,1},{3,2},{5,4},{6,5},{7,6},{9,8},{10,9},{11,10},{13,12},{... | collective-permute-start | bytes 49160 | tf_op jit(solution)/shard_map/while/body/eval_jaxpr/ppermute | solution.py:18
  31.9 6.6 %collective-permute-start.1 = (f32[1,8,4,128]{3,2,1,0:T(4,128)S(1)}, f32[1,8,4,128]{3,2,1,0:T(4,128)S(1)}, u32[]{:S(2)}, u32[]{:S(2)}) collective-permute-start(f32[1,8,4,128]{3,2,1,0:T(4,128)S(1)} %pad_maximum_fusion.6), channel_id=1, source_target_pairs={{0,1},{1,2},{2,3},{4,5},{5,6},{6,7},{8,9},{9,10},{10,11},{12,13},{... | collective-permute-start | bytes 49160 | tf_op jit(solution)/shard_map/while/body/eval_jaxpr/ppermute | solution.py:15
  35.4 5.6 %collective-permute-start = (f32[1,8,4,128]{3,2,1,0:T(4,128)S(1)}, f32[1,8,4,128]{3,2,1,0:T(4,128)S(1)}, u32[]{:S(2)}, u32[]{:S(2)}) collective-permute-start(f32[1,8,4,128]{3,2,1,0:T(4,128)S(1)} %pad_maximum_fusion.6), channel_id=1, source_target_pairs={{1,0},{2,1},{3,2},{5,4},{6,5},{7,6},{9,8},{10,9},{11,10},{13,12},{... | collective-permute-start | bytes 49160 | tf_op jit(solution)/shard_map/while/body/eval_jaxpr/ppermute | solution.py:18
  47.3 6.6 %collective-permute-start.1 = (f32[1,8,4,128]{3,2,1,0:T(4,128)S(1)}, f32[1,8,4,128]{3,2,1,0:T(4,128)S(1)}, u32[]{:S(2)}, u32[]{:S(2)}) collective-permute-start(f32[1,8,4,128]{3,2,1,0:T(4,128)S(1)} %pad_maximum_fusion.6), channel_id=1, source_target_pairs={{0,1},{1,2},{2,3},{4,5},{5,6},{6,7},{8,9},{9,10},{10,11},{12,13},{... | collective-permute-start | bytes 49160 | tf_op jit(solution)/shard_map/while/body/eval_jaxpr/ppermute | solution.py:15
  50.8 5.6 %collective-permute-start = (f32[1,8,4,128]{3,2,1,0:T(4,128)S(1)}, f32[1,8,4,128]{3,2,1,0:T(4,128)S(1)}, u32[]{:S(2)}, u32[]{:S(2)}) collective-permute-start(f32[1,8,4,128]{3,2,1,0:T(4,128)S(1)} %pad_maximum_fusion.6), channel_id=1, source_target_pairs={{1,0},{2,1},{3,2},{5,4},{6,5},{7,6},{9,8},{10,9},{11,10},{13,12},{... | collective-permute-start | bytes 49160 | tf_op jit(solution)/shard_map/while/body/eval_jaxpr/ppermute | solution.py:18
  62.7 5.1 %collective-permute-start.1 = (f32[1,8,4,128]{3,2,1,0:T(4,128)S(1)}, f32[1,8,4,128]{3,2,1,0:T(4,128)S(1)}, u32[]{:S(2)}, u32[]{:S(2)}) collective-permute-start(f32[1,8,4,128]{3,2,1,0:T(4,128)S(1)} %pad_maximum_fusion.6), channel_id=1, source_target_pairs={{0,1},{1,2},{2,3},{4,5},{5,6},{6,7},{8,9},{9,10},{10,11},{12,13},{... | collective-permute-start | bytes 49160 | tf_op jit(solution)/shard_map/while/body/eval_jaxpr/ppermute | solution.py:15
  64.7 5.6 %collective-permute-start = (f32[1,8,4,128]{3,2,1,0:T(4,128)S(1)}, f32[1,8,4,128]{3,2,1,0:T(4,128)S(1)}, u32[]{:S(2)}, u32[]{:S(2)}) collective-permute-start(f32[1,8,4,128]{3,2,1,0:T(4,128)S(1)} %pad_maximum_fusion.6), channel_id=1, source_target_pairs={{1,0},{2,1},{3,2},{5,4},{6,5},{7,6},{9,8},{10,9},{11,10},{13,12},{... | collective-permute-start | bytes 49160 | tf_op jit(solution)/shard_map/while/body/eval_jaxpr/ppermute | solution.py:18
  76.5 5.1 %collective-permute-start.1 = (f32[1,8,4,128]{3,2,1,0:T(4,128)S(1)}, f32[1,8,4,128]{3,2,1,0:T(4,128)S(1)}, u32[]{:S(2)}, u32[]{:S(2)}) collective-permute-start(f32[1,8,4,128]{3,2,1,0:T(4,128)S(1)} %pad_maximum_fusion.6), channel_id=1, source_target_pairs={{0,1},{1,2},{2,3},{4,5},{5,6},{6,7},{8,9},{9,10},{10,11},{12,13},{... | collective-permute-start | bytes 49160 | tf_op jit(solution)/shard_map/while/body/eval_jaxpr/ppermute | solution.py:15
  78.5 5.6 %collective-permute-start = (f32[1,8,4,128]{3,2,1,0:T(4,128)S(1)}, f32[1,8,4,128]{3,2,1,0:T(4,128)S(1)}, u32[]{:S(2)}, u32[]{:S(2)}) collective-permute-start(f32[1,8,4,128]{3,2,1,0:T(4,128)S(1)} %pad_maximum_fusion.6), channel_id=1, source_target_pairs={{1,0},{2,1},{3,2},{5,4},{6,5},{7,6},{9,8},{10,9},{11,10},{13,12},{... | collective-permute-start | bytes 49160 | tf_op jit(solution)/shard_map/while/body/eval_jaxpr/ppermute | solution.py:18
  90.4 5.1 %collective-permute-start.1 = (f32[1,8,4,128]{3,2,1,0:T(4,128)S(1)}, f32[1,8,4,128]{3,2,1,0:T(4,128)S(1)}, u32[]{:S(2)}, u32[]{:S(2)}) collective-permute-start(f32[1,8,4,128]{3,2,1,0:T(4,128)S(1)} %pad_maximum_fusion.6), channel_id=1, source_target_pairs={{0,1},{1,2},{2,3},{4,5},{5,6},{6,7},{8,9},{9,10},{10,11},{12,13},{... | collective-permute-start | bytes 49160 | tf_op jit(solution)/shard_map/while/body/eval_jaxpr/ppermute | solution.py:15
  92.4 5.6 %collective-permute-start = (f32[1,8,4,128]{3,2,1,0:T(4,128)S(1)}, f32[1,8,4,128]{3,2,1,0:T(4,128)S(1)}, u32[]{:S(2)}, u32[]{:S(2)}) collective-permute-start(f32[1,8,4,128]{3,2,1,0:T(4,128)S(1)} %pad_maximum_fusion.6), channel_id=1, source_target_pairs={{1,0},{2,1},{3,2},{5,4},{6,5},{7,6},{9,8},{10,9},{11,10},{13,12},{... | collective-permute-start | bytes 49160 | tf_op jit(solution)/shard_map/while/body/eval_jaxpr/ppermute | solution.py:18
  104.3 5.1 %collective-permute-start.1 = (f32[1,8,4,128]{3,2,1,0:T(4,128)S(1)}, f32[1,8,4,128]{3,2,1,0:T(4,128)S(1)}, u32[]{:S(2)}, u32[]{:S(2)}) collective-permute-start(f32[1,8,4,128]{3,2,1,0:T(4,128)S(1)} %pad_maximum_fusion.6), channel_id=1, source_target_pairs={{0,1},{1,2},{2,3},{4,5},{5,6},{6,7},{8,9},{9,10},{10,11},{12,13},{... | collective-permute-start | bytes 49160 | tf_op jit(solution)/shard_map/while/body/eval_jaxpr/ppermute | solution.py:15
  106.3 5.6 %collective-permute-start = (f32[1,8,4,128]{3,2,1,0:T(4,128)S(1)}, f32[1,8,4,128]{3,2,1,0:T(4,128)S(1)}, u32[]{:S(2)}, u32[]{:S(2)}) collective-permute-start(f32[1,8,4,128]{3,2,1,0:T(4,128)S(1)} %pad_maximum_fusion.6), channel_id=1, source_target_pairs={{1,0},{2,1},{3,2},{5,4},{6,5},{7,6},{9,8},{10,9},{11,10},{13,12},{... | collective-permute-start | bytes 49160 | tf_op jit(solution)/shard_map/while/body/eval_jaxpr/ppermute | solution.py:18
  118.1 5.1 %collective-permute-start.1 = (f32[1,8,4,128]{3,2,1,0:T(4,128)S(1)}, f32[1,8,4,128]{3,2,1,0:T(4,128)S(1)}, u32[]{:S(2)}, u32[]{:S(2)}) collective-permute-start(f32[1,8,4,128]{3,2,1,0:T(4,128)S(1)} %pad_maximum_fusion.6), channel_id=1, source_target_pairs={{0,1},{1,2},{2,3},{4,5},{5,6},{6,7},{8,9},{9,10},{10,11},{12,13},{... | collective-permute-start | bytes 49160 | tf_op jit(solution)/shard_map/while/body/eval_jaxpr/ppermute | solution.py:15
  120.1 5.6 %collective-permute-start = (f32[1,8,4,128]{3,2,1,0:T(4,128)S(1)}, f32[1,8,4,128]{3,2,1,0:T(4,128)S(1)}, u32[]{:S(2)}, u32[]{:S(2)}) collective-permute-start(f32[1,8,4,128]{3,2,1,0:T(4,128)S(1)} %pad_maximum_fusion.6), channel_id=1, source_target_pairs={{1,0},{2,1},{3,2},{5,4},{6,5},{7,6},{9,8},{10,9},{11,10},{13,12},{... | collective-permute-start | bytes 49160 | tf_op jit(solution)/shard_map/while/body/eval_jaxpr/ppermute | solution.py:18
  132.0 5.1 %collective-permute-start.1 = (f32[1,8,4,128]{3,2,1,0:T(4,128)S(1)}, f32[1,8,4,128]{3,2,1,0:T(4,128)S(1)}, u32[]{:S(2)}, u32[]{:S(2)}) collective-permute-start(f32[1,8,4,128]{3,2,1,0:T(4,128)S(1)} %pad_maximum_fusion.6), channel_id=1, source_target_pairs={{0,1},{1,2},{2,3},{4,5},{5,6},{6,7},{8,9},{9,10},{10,11},{12,13},{... | collective-permute-start | bytes 49160 | tf_op jit(solution)/shard_map/while/body/eval_jaxpr/ppermute | solution.py:15
  134.0 5.6 %collective-permute-start = (f32[1,8,4,128]{3,2,1,0:T(4,128)S(1)}, f32[1,8,4,128]{3,2,1,0:T(4,128)S(1)}, u32[]{:S(2)}, u32[]{:S(2)}) collective-permute-start(f32[1,8,4,128]{3,2,1,0:T(4,128)S(1)} %pad_maximum_fusion.6), channel_id=1, source_target_pairs={{1,0},{2,1},{3,2},{5,4},{6,5},{7,6},{9,8},{10,9},{11,10},{13,12},{... | collective-permute-start | bytes 49160 | tf_op jit(solution)/shard_map/while/body/eval_jaxpr/ppermute | solution.py:18
  145.8 5.1 %collective-permute-start.1 = (f32[1,8,4,128]{3,2,1,0:T(4,128)S(1)}, f32[1,8,4,128]{3,2,1,0:T(4,128)S(1)}, u32[]{:S(2)}, u32[]{:S(2)}) collective-permute-start(f32[1,8,4,128]{3,2,1,0:T(4,128)S(1)} %pad_maximum_fusion.6), channel_id=1, source_target_pairs={{0,1},{1,2},{2,3},{4,5},{5,6},{6,7},{8,9},{9,10},{10,11},{12,13},{... | collective-permute-start | bytes 49160 | tf_op jit(solution)/shard_map/while/body/eval_jaxpr/ppermute | solution.py:15
  147.8 5.6 %collective-permute-start = (f32[1,8,4,128]{3,2,1,0:T(4,128)S(1)}, f32[1,8,4,128]{3,2,1,0:T(4,128)S(1)}, u32[]{:S(2)}, u32[]{:S(2)}) collective-permute-start(f32[1,8,4,128]{3,2,1,0:T(4,128)S(1)} %pad_maximum_fusion.6), channel_id=1, source_target_pairs={{1,0},{2,1},{3,2},{5,4},{6,5},{7,6},{9,8},{10,9},{11,10},{13,12},{... | collective-permute-start | bytes 49160 | tf_op jit(solution)/shard_map/while/body/eval_jaxpr/ppermute | solution.py:18
  159.7 5.1 %collective-permute-start.1 = (f32[1,8,4,128]{3,2,1,0:T(4,128)S(1)}, f32[1,8,4,128]{3,2,1,0:T(4,128)S(1)}, u32[]{:S(2)}, u32[]{:S(2)}) collective-permute-start(f32[1,8,4,128]{3,2,1,0:T(4,128)S(1)} %pad_maximum_fusion.6), channel_id=1, source_target_pairs={{0,1},{1,2},{2,3},{4,5},{5,6},{6,7},{8,9},{9,10},{10,11},{12,13},{... | collective-permute-start | bytes 49160 | tf_op jit(solution)/shard_map/while/body/eval_jaxpr/ppermute | solution.py:15
  161.7 5.6 %collective-permute-start = (f32[1,8,4,128]{3,2,1,0:T(4,128)S(1)}, f32[1,8,4,128]{3,2,1,0:T(4,128)S(1)}, u32[]{:S(2)}, u32[]{:S(2)}) collective-permute-start(f32[1,8,4,128]{3,2,1,0:T(4,128)S(1)} %pad_maximum_fusion.6), channel_id=1, source_target_pairs={{1,0},{2,1},{3,2},{5,4},{6,5},{7,6},{9,8},{10,9},{11,10},{13,12},{... | collective-permute-start | bytes 49160 | tf_op jit(solution)/shard_map/while/body/eval_jaxpr/ppermute | solution.py:18
  173.6 5.1 %collective-permute-start.1 = (f32[1,8,4,128]{3,2,1,0:T(4,128)S(1)}, f32[1,8,4,128]{3,2,1,0:T(4,128)S(1)}, u32[]{:S(2)}, u32[]{:S(2)}) collective-permute-start(f32[1,8,4,128]{3,2,1,0:T(4,128)S(1)} %pad_maximum_fusion.6), channel_id=1, source_target_pairs={{0,1},{1,2},{2,3},{4,5},{5,6},{6,7},{8,9},{9,10},{10,11},{12,13},{... | collective-permute-start | bytes 49160 | tf_op jit(solution)/shard_map/while/body/eval_jaxpr/ppermute | solution.py:15
  175.6 5.6 %collective-permute-start = (f32[1,8,4,128]{3,2,1,0:T(4,128)S(1)}, f32[1,8,4,128]{3,2,1,0:T(4,128)S(1)}, u32[]{:S(2)}, u32[]{:S(2)}) collective-permute-start(f32[1,8,4,128]{3,2,1,0:T(4,128)S(1)} %pad_maximum_fusion.6), channel_id=1, source_target_pairs={{1,0},{2,1},{3,2},{5,4},{6,5},{7,6},{9,8},{10,9},{11,10},{13,12},{... | collective-permute-start | bytes 49160 | tf_op jit(solution)/shard_map/while/body/eval_jaxpr/ppermute | solution.py:18
  187.1 1.7 copy-start
  263.7 14.2 %copy-start.3 = (f32[1,8,128,128]{3,2,1,0:T(8,128)S(1)}, f32[1,8,128,128]{3,2,1,0:T(8,128)}, u32[]{:S(2)}) copy-start(f32[1,8,128,128]{3,2,1,0:T(8,128)} %param.12) | copy-start | bytes 1572868
  266.5 12.3 %copy-start.5 = (f32[1,8,128,128]{3,2,1,0:T(8,128)}, f32[1,8,128,128]{3,2,1,0:T(8,128)S(1)}, u32[]{:S(2)}) copy-start(f32[1,8,128,128]{3,2,1,0:T(8,128)S(1)} %add.163) | copy-start | bytes 1572868
  266.5 11.4 %collective-permute-start.2 = (f32[8,128,128]{2,1,0:T(8,128)S(1)}, f32[8,128,128]{2,1,0:T(8,128)S(1)}, u32[]{:S(2)}, u32[]{:S(2)}) collective-permute-start(f32[8,128,128]{2,1,0:T(8,128)S(1)} %bitcast.111), channel_id=1, source_target_pairs={{0,4},{4,8},{8,12},{12,16},{16,20},{20,24},{24,28},{1,5},{5,9},{9,... | collective-permute-start | bytes 1572872 | tf_op jit(solution)/shard_map/ppermute | solution.py:31
Sparse Core Ops, SparseCore 0:
  11.0 54.4 all-reduce.5
  191.3 25.8 all-gather.1
where the time goes:
time: 288 us; the launch traced here: 286 us
  local copies, waits for them, and re-layouts  79.5 us (28%)
  waiting for transfers between devices  66.1 us (23%)
  starting transfers between devices  46.1 us (16%)
  other arithmetic  40.4 us (14%)
  matrix products  38 us (13%)
  between operations  14.3 us (5%)
    mul x12, other arithmetic, advance(): open_cells * (current + strength * diffusivity * laplace - 0.5 * transport)  35.6 us
    ppermute x12, waiting for transfers between devices, padded(): lax.ppermute(lax.slice_in_dim(block, 0, width, axis=dim), axis, backward)  30.8 us
    ppermute x12, starting transfers between devices, padded(): lax.ppermute(lax.slice_in_dim(block, block.shape[dim] - width, None, axis...  28.3 us
    all_gather x1, waiting for transfers between devices, on_device(): every_jump = lax.all_gather(coarse_jump, 'tm', axis=0, tiled=True)  26 us
    dot_general x10, matrix products, apply_coarse(): jnp.einsum('...tik,tlk->...til', mixed_x, matrix_y, precision=exact_preci...  24.6 us
    ppermute x12, starting transfers between devices, padded(): lax.ppermute(lax.slice_in_dim(block, 0, width, axis=dim), axis, backward)  15.5 us
    dot_general x10, matrix products, apply_coarse(): jnp.einsum('tij,...tjk->...tik', matrix_x, coarse_values, precision=exact...  13.5 us
    dynamic_update_slice x8, local copies, waits for them, and re-layouts, on_device(): last_state, history = lax.scan(sweep, first_coarse, every_jump)  13.4 us
  transfers between devices with their start and end apart: 27, of which 14 were waited for; matrix products, arithmetic and copies ran while one was open for 37% of the time, Pallas kernels for 0%

commit v1 on v0

--- a/solution.py
+++ b/solution.py
@@ -81,7 +81,9 @@
     correction = fine_ends - prolong(apply_coarse(restrict(starts), coarse_x, coarse_y))
     coarse_jump = restrict(correction)
     first_coarse = spread(restrict(starts[0]), "tm", 0)
-    every_jump = lax.all_gather(coarse_jump, "tm", axis=0, tiled=True)
+    every_jump = jnp.concatenate(
+        lax.all_to_all(jnp.stack([coarse_jump] * lax.axis_size("tm")), "tm", 0, 0), axis=0
+    )
 
     def sweep(state_now, jump):
         return (apply_coarse(state_now, coarse_x, coarse_y) + jump, state_now)

time: 288 us -> 328 us (1.14)
  waiting for transfers between devices: 66.1 us -> 100 us
  starting transfers between devices: 46.1 us -> 50.9 us
    psum x1, waiting for transfers between devices: 0.02 us -> 60.2 us  [spread(): return lax.psum(kept, axis)]
    all_gather x1 -> x0, waiting for transfers between devices: 26 us -> none  [on_device(): every_jump = lax.all_gather(coarse_jump, 'tm', axis=0, tiled=True)]
    all_to_all x0 -> x1, starting transfers between devices: none -> 4.87 us  [on_device(): lax.all_to_all(jnp.stack([coarse_jump] * lax.axis_size('tm')), 'tm', 0, 0)]
  transfers between devices with their start and end apart: 27 -> 27, of which waited for: 14 -> 14; matrix products, arithmetic and copies ran while one was open for 37% -> 7% of each run, Pallas kernels for 0% -> 0%
where the time goes in v1:
time: 328 us; the launch traced here: 325 us
  waiting for transfers between devices  100 us (30%)
  local copies, waits for them, and re-layouts  82.5 us (25%)
  starting transfers between devices  50.9 us (16%)
  other arithmetic  38.6 us (12%)
  matrix products  37.9 us (12%)
  between operations  14.3 us (4%)
    psum x1, waiting for transfers between devices, spread(): return lax.psum(kept, axis)  60.2 us
    mul x12, other arithmetic, advance(): open_cells * (current + strength * diffusivity * laplace - 0.5 * transport)  34.5 us
    ppermute x12, waiting for transfers between devices, padded(): lax.ppermute(lax.slice_in_dim(block, 0, width, axis=dim), axis, backward)  30.5 us
    ppermute x12, starting transfers between devices, padded(): lax.ppermute(lax.slice_in_dim(block, block.shape[dim] - width, None, axis...  28.6 us
    dot_general x10, matrix products, apply_coarse(): jnp.einsum('...tik,tlk->...til', mixed_x, matrix_y, precision=exact_preci...  24.6 us
    ppermute x12, starting transfers between devices, padded(): lax.ppermute(lax.slice_in_dim(block, 0, width, axis=dim), axis, backward)  15.5 us
    dynamic_update_slice x8, local copies, waits for them, and re-layouts, on_device(): last_state, history = lax.scan(sweep, first_coarse, every_jump)  13.4 us
    dot_general x10, matrix products, apply_coarse(): jnp.einsum('tij,...tjk->...tik', matrix_x, coarse_values, precision=exact...  13.3 us
  transfers between devices with their start and end apart: 27, of which 14 were waited for; matrix products, arithmetic and copies ran while one was open for 7% of the time, Pallas kernels for 0%

profile of v1, /device:TPU:4, one launch (start us, length us, event | category | flops | bytes accessed | tf_op | source)
XLA Modules:
  0.0 325.5 jit_solution(14391470796715977345)
XLA Ops:
  16.2 170.0 %while.25 = (s32[]{:T(128)}, f32[1,8,128,128]{2,1,3,0:T(8,128)S(1)}, f32[8,128,128]{1,0,2:T(8,128)}, f32[12]{0:T(128)S(1)}, f32[8,128,128]{1,0,2:T(8,128)}, /*in...) while((s32[]{:T(128)}, ...), condition=%wide.region_2.3_spmd, body=%wide.region_1.2_spmd.sunk | while | flops 2710714 | bytes 10800037 | solution.py:80
  16.5 3.5 %collective-permute-start.1 = (f32[1,8,4,128]{3,2,1,0:T(4,128)S(1)}, f32[1,8,4,128]{3,2,1,0:T(4,128)S(1)}, u32[]{:S(2)}, u32[]{:S(2)}) collective-permute-start(f32[1,8,4,128]{3,2,1,0:T(4,128)S(1)} %pad_maximum_fusion.6), channel_id=1, source_target_pairs={{0,1},{1,2},{2,3},{4,5},{5,6},{6,7},{8,9},{9,10},{10,11},{12,13},{... | collective-permute-start | bytes 49160 | tf_op jit(solution)/shard_map/while/body/eval_jaxpr/ppermute | solution.py:15
  23.1 2.5 collective-permute-done
  28.6 2.9 fusion.60
  31.8 3.5 %collective-permute-start.1 = (f32[1,8,4,128]{3,2,1,0:T(4,128)S(1)}, f32[1,8,4,128]{3,2,1,0:T(4,128)S(1)}, u32[]{:S(2)}, u32[]{:S(2)}) collective-permute-start(f32[1,8,4,128]{3,2,1,0:T(4,128)S(1)} %pad_maximum_fusion.6), channel_id=1, source_target_pairs={{0,1},{1,2},{2,3},{4,5},{5,6},{6,7},{8,9},{9,10},{10,11},{12,13},{... | collective-permute-start | bytes 49160 | tf_op jit(solution)/shard_map/while/body/eval_jaxpr/ppermute | solution.py:15
  38.4 2.5 collective-permute-done
  43.9 2.9 fusion.60
  47.1 3.5 %collective-permute-start.1 = (f32[1,8,4,128]{3,2,1,0:T(4,128)S(1)}, f32[1,8,4,128]{3,2,1,0:T(4,128)S(1)}, u32[]{:S(2)}, u32[]{:S(2)}) collective-permute-start(f32[1,8,4,128]{3,2,1,0:T(4,128)S(1)} %pad_maximum_fusion.6), channel_id=1, source_target_pairs={{0,1},{1,2},{2,3},{4,5},{5,6},{6,7},{8,9},{9,10},{10,11},{12,13},{... | collective-permute-start | bytes 49160 | tf_op jit(solution)/shard_map/while/body/eval_jaxpr/ppermute | solution.py:15
  53.7 2.5 collective-permute-done
  59.2 2.9 fusion.60
  62.3 2.0 collective-permute-start.1
  67.5 2.5 collective-permute-done
  73.0 2.9 fusion.60
  76.1 2.0 collective-permute-start.1
  81.3 2.5 collective-permute-done
  86.8 2.9 fusion.60
  89.9 2.0 collective-permute-start.1
  95.1 2.5 collective-permute-done
  100.6 2.9 fusion.60
  103.7 2.0 collective-permute-start.1
  108.9 2.5 collective-permute-done
  114.4 2.9 fusion.60
  117.5 2.0 collective-permute-start.1
  122.7 2.5 collective-permute-done
  128.1 2.9 fusion.60
  131.3 2.0 collective-permute-start.1
  136.4 2.5 collective-permute-done
  141.9 2.9 fusion.60
  145.1 2.0 collective-permute-start.1
  150.2 2.5 collective-permute-done
  155.7 2.9 fusion.60
  158.9 2.0 collective-permute-start.1
  164.0 2.5 collective-permute-done
  169.5 2.9 fusion.60
  177.8 2.5 collective-permute-done
  183.3 2.9 fusion.60
  191.2 4.9 %all-to-all-start = ((f32[8,1,8,64,128]{4,3,2,1,0:T(8,128)}), f32[8,1,8,64,128]{4,3,2,1,0:T(8,128)}, u32[]{:S(2)}, u32[]{:S(2)}) async-start(f32[8,1,8,64,128]{4,3,2,1,0:T(8,128)} %stack.9), calls=%async_computation | async-start | bytes 4194304 | tf_op jit(solution)/shard_map/all_to_all | solution.py:85
  197.1 60.2 %all-reduce.6.cloned.1.call-done = f32[8,64,128]{2,1,0:T(8,128)} async-done(((f32[8,64,128]{2,1,0:T(8,128)}), f32[8,64,128]{2,1,0:T(8,128)}) %all-reduce.6.cloned.1.call-update) | async-done | bytes 262160 | tf_op jit(solution)/shard_map/psum | solution.py:25
  257.2 46.4 %while.26 = (s32[]{:T(128)}, f32[8,64,128]{2,1,0:T(8,128)}, f32[8,8,64,128]{3,2,1,0:T(8,128)}, f32[8,64,64]{2,1,0:T(8,128)S(1)}, f32[8,128,128]{2,1,0:T(8,128)S(1)}, /*index=5*/f32[8,8,64,128]{3,2,1,0:T(8,128)}, s32[]{:T(128)}) while((s32[]{:T(128)}, f32[8,64,128]{2,1,0:T(8,128)}, f32[8,8,64,128]{3,2,1,0:T(8,128)}, ...), condition=%wide.region_4.5_spmd, body=%wide.region_3.4_spmd.sunk | while | flops 151060480 | bytes 2490461 | solution.py:91
  260.3 2.8 convolution_add_fusion.2
  266.1 2.8 convolution_add_fusion.2
  271.9 2.8 convolution_add_fusion.2
  277.7 2.8 convolution_add_fusion.2
  283.5 2.8 convolution_add_fusion.2
  289.3 2.8 convolution_add_fusion.2
  295.1 2.8 convolution_add_fusion.2
  300.9 2.8 convolution_add_fusion.2
  308.3 9.5 %collective-permute-done.2 = f32[8,128,128]{2,1,0:T(8,128)S(1)} collective-permute-done((f32[8,128,128]{2,1,0:T(8,128)S(1)}, f32[8,128,128]{2,1,0:T(8,128)S(1)}, u32[]{:S(2)}, u32[]{:S(2)}) %collective-permute-start.2) | collective-permute-done | bytes 524320 | tf_op jit(solution)/shard_map/ppermute | solution.py:31
  (283 shorter events, 121.6 us)
Async XLA Ops:
  7.2 4.9 %copy-start.5 = (f32[8,128,128]{2,1,0:T(8,128)S(1)}, f32[8,128,128]{2,1,0:T(8,128)}, u32[]{:S(2)}) copy-start(f32[8,128,128]{2,1,0:T(8,128)} %param.13) | copy-start | bytes 1572868
  7.2 5.9 %copy-start.6 = (s32[8,128,128]{2,1,0:T(8,128)S(1)}, s32[8,128,128]{2,1,0:T(8,128)}, u32[]{:S(2)}) copy-start(s32[8,128,128]{2,1,0:T(8,128)} %param.15) | copy-start | bytes 1572868
  10.7 3.5 %copy-start.3 = (f32[2,8,128,128]{3,2,1,0:T(8,128)S(1)}, f32[2,8,128,128]{3,2,1,0:T(8,128)}, u32[]{:S(2)}) copy-start(f32[2,8,128,128]{3,2,1,0:T(8,128)} %param.14) | copy-start | bytes 3145732
  14.1 2.1 copy-start.7
  14.1 2.1 copy-start.8
  16.2 170.2 %copy-start.1 = (f32[8,64,64]{2,1,0:T(8,128)S(1)}, f32[8,64,64]{2,1,0:T(8,128)}, u32[]{:S(2)}) copy-start(f32[8,64,64]{2,1,0:T(8,128)} %param.18) | copy-start | bytes 393220
  16.5 6.6 %collective-permute-start.1 = (f32[1,8,4,128]{3,2,1,0:T(4,128)S(1)}, f32[1,8,4,128]{3,2,1,0:T(4,128)S(1)}, u32[]{:S(2)}, u32[]{:S(2)}) collective-permute-start(f32[1,8,4,128]{3,2,1,0:T(4,128)S(1)} %pad_maximum_fusion.6), channel_id=1, source_target_pairs={{0,1},{1,2},{2,3},{4,5},{5,6},{6,7},{8,9},{9,10},{10,11},{12,13},{... | collective-permute-start | bytes 49160 | tf_op jit(solution)/shard_map/while/body/eval_jaxpr/ppermute | solution.py:15
  20.0 5.6 %collective-permute-start = (f32[1,8,4,128]{3,2,1,0:T(4,128)S(1)}, f32[1,8,4,128]{3,2,1,0:T(4,128)S(1)}, u32[]{:S(2)}, u32[]{:S(2)}) collective-permute-start(f32[1,8,4,128]{3,2,1,0:T(4,128)S(1)} %pad_maximum_fusion.6), channel_id=1, source_target_pairs={{1,0},{2,1},{3,2},{5,4},{6,5},{7,6},{9,8},{10,9},{11,10},{13,12},{... | collective-permute-start | bytes 49160 | tf_op jit(solution)/shard_map/while/body/eval_jaxpr/ppermute | solution.py:18
  31.8 6.6 %collective-permute-start.1 = (f32[1,8,4,128]{3,2,1,0:T(4,128)S(1)}, f32[1,8,4,128]{3,2,1,0:T(4,128)S(1)}, u32[]{:S(2)}, u32[]{:S(2)}) collective-permute-start(f32[1,8,4,128]{3,2,1,0:T(4,128)S(1)} %pad_maximum_fusion.6), channel_id=1, source_target_pairs={{0,1},{1,2},{2,3},{4,5},{5,6},{6,7},{8,9},{9,10},{10,11},{12,13},{... | collective-permute-start | bytes 49160 | tf_op jit(solution)/shard_map/while/body/eval_jaxpr/ppermute | solution.py:15
  35.3 5.6 %collective-permute-start = (f32[1,8,4,128]{3,2,1,0:T(4,128)S(1)}, f32[1,8,4,128]{3,2,1,0:T(4,128)S(1)}, u32[]{:S(2)}, u32[]{:S(2)}) collective-permute-start(f32[1,8,4,128]{3,2,1,0:T(4,128)S(1)} %pad_maximum_fusion.6), channel_id=1, source_target_pairs={{1,0},{2,1},{3,2},{5,4},{6,5},{7,6},{9,8},{10,9},{11,10},{13,12},{... | collective-permute-start | bytes 49160 | tf_op jit(solution)/shard_map/while/body/eval_jaxpr/ppermute | solution.py:18
  47.1 6.6 %collective-permute-start.1 = (f32[1,8,4,128]{3,2,1,0:T(4,128)S(1)}, f32[1,8,4,128]{3,2,1,0:T(4,128)S(1)}, u32[]{:S(2)}, u32[]{:S(2)}) collective-permute-start(f32[1,8,4,128]{3,2,1,0:T(4,128)S(1)} %pad_maximum_fusion.6), channel_id=1, source_target_pairs={{0,1},{1,2},{2,3},{4,5},{5,6},{6,7},{8,9},{9,10},{10,11},{12,13},{... | collective-permute-start | bytes 49160 | tf_op jit(solution)/shard_map/while/body/eval_jaxpr/ppermute | solution.py:15
  50.6 5.6 %collective-permute-start = (f32[1,8,4,128]{3,2,1,0:T(4,128)S(1)}, f32[1,8,4,128]{3,2,1,0:T(4,128)S(1)}, u32[]{:S(2)}, u32[]{:S(2)}) collective-permute-start(f32[1,8,4,128]{3,2,1,0:T(4,128)S(1)} %pad_maximum_fusion.6), channel_id=1, source_target_pairs={{1,0},{2,1},{3,2},{5,4},{6,5},{7,6},{9,8},{10,9},{11,10},{13,12},{... | collective-permute-start | bytes 49160 | tf_op jit(solution)/shard_map/while/body/eval_jaxpr/ppermute | solution.py:18
  62.3 5.1 %collective-permute-start.1 = (f32[1,8,4,128]{3,2,1,0:T(4,128)S(1)}, f32[1,8,4,128]{3,2,1,0:T(4,128)S(1)}, u32[]{:S(2)}, u32[]{:S(2)}) collective-permute-start(f32[1,8,4,128]{3,2,1,0:T(4,128)S(1)} %pad_maximum_fusion.6), channel_id=1, source_target_pairs={{0,1},{1,2},{2,3},{4,5},{5,6},{6,7},{8,9},{9,10},{10,11},{12,13},{... | collective-permute-start | bytes 49160 | tf_op jit(solution)/shard_map/while/body/eval_jaxpr/ppermute | solution.py:15
  64.4 5.6 %collective-permute-start = (f32[1,8,4,128]{3,2,1,0:T(4,128)S(1)}, f32[1,8,4,128]{3,2,1,0:T(4,128)S(1)}, u32[]{:S(2)}, u32[]{:S(2)}) collective-permute-start(f32[1,8,4,128]{3,2,1,0:T(4,128)S(1)} %pad_maximum_fusion.6), channel_id=1, source_target_pairs={{1,0},{2,1},{3,2},{5,4},{6,5},{7,6},{9,8},{10,9},{11,10},{13,12},{... | collective-permute-start | bytes 49160 | tf_op jit(solution)/shard_map/while/body/eval_jaxpr/ppermute | solution.py:18
  76.1 5.1 %collective-permute-start.1 = (f32[1,8,4,128]{3,2,1,0:T(4,128)S(1)}, f32[1,8,4,128]{3,2,1,0:T(4,128)S(1)}, u32[]{:S(2)}, u32[]{:S(2)}) collective-permute-start(f32[1,8,4,128]{3,2,1,0:T(4,128)S(1)} %pad_maximum_fusion.6), channel_id=1, source_target_pairs={{0,1},{1,2},{2,3},{4,5},{5,6},{6,7},{8,9},{9,10},{10,11},{12,13},{... | collective-permute-start | bytes 49160 | tf_op jit(solution)/shard_map/while/body/eval_jaxpr/ppermute | solution.py:15
  78.2 5.6 %collective-permute-start = (f32[1,8,4,128]{3,2,1,0:T(4,128)S(1)}, f32[1,8,4,128]{3,2,1,0:T(4,128)S(1)}, u32[]{:S(2)}, u32[]{:S(2)}) collective-permute-start(f32[1,8,4,128]{3,2,1,0:T(4,128)S(1)} %pad_maximum_fusion.6), channel_id=1, source_target_pairs={{1,0},{2,1},{3,2},{5,4},{6,5},{7,6},{9,8},{10,9},{11,10},{13,12},{... | collective-permute-start | bytes 49160 | tf_op jit(solution)/shard_map/while/body/eval_jaxpr/ppermute | solution.py:18
  89.9 5.1 %collective-permute-start.1 = (f32[1,8,4,128]{3,2,1,0:T(4,128)S(1)}, f32[1,8,4,128]{3,2,1,0:T(4,128)S(1)}, u32[]{:S(2)}, u32[]{:S(2)}) collective-permute-start(f32[1,8,4,128]{3,2,1,0:T(4,128)S(1)} %pad_maximum_fusion.6), channel_id=1, source_target_pairs={{0,1},{1,2},{2,3},{4,5},{5,6},{6,7},{8,9},{9,10},{10,11},{12,13},{... | collective-permute-start | bytes 49160 | tf_op jit(solution)/shard_map/while/body/eval_jaxpr/ppermute | solution.py:15
  92.0 5.6 %collective-permute-start = (f32[1,8,4,128]{3,2,1,0:T(4,128)S(1)}, f32[1,8,4,128]{3,2,1,0:T(4,128)S(1)}, u32[]{:S(2)}, u32[]{:S(2)}) collective-permute-start(f32[1,8,4,128]{3,2,1,0:T(4,128)S(1)} %pad_maximum_fusion.6), channel_id=1, source_target_pairs={{1,0},{2,1},{3,2},{5,4},{6,5},{7,6},{9,8},{10,9},{11,10},{13,12},{... | collective-permute-start | bytes 49160 | tf_op jit(solution)/shard_map/while/body/eval_jaxpr/ppermute | solution.py:18
  103.7 5.1 %collective-permute-start.1 = (f32[1,8,4,128]{3,2,1,0:T(4,128)S(1)}, f32[1,8,4,128]{3,2,1,0:T(4,128)S(1)}, u32[]{:S(2)}, u32[]{:S(2)}) collective-permute-start(f32[1,8,4,128]{3,2,1,0:T(4,128)S(1)} %pad_maximum_fusion.6), channel_id=1, source_target_pairs={{0,1},{1,2},{2,3},{4,5},{5,6},{6,7},{8,9},{9,10},{10,11},{12,13},{... | collective-permute-start | bytes 49160 | tf_op jit(solution)/shard_map/while/body/eval_jaxpr/ppermute | solution.py:15
  105.8 5.6 %collective-permute-start = (f32[1,8,4,128]{3,2,1,0:T(4,128)S(1)}, f32[1,8,4,128]{3,2,1,0:T(4,128)S(1)}, u32[]{:S(2)}, u32[]{:S(2)}) collective-permute-start(f32[1,8,4,128]{3,2,1,0:T(4,128)S(1)} %pad_maximum_fusion.6), channel_id=1, source_target_pairs={{1,0},{2,1},{3,2},{5,4},{6,5},{7,6},{9,8},{10,9},{11,10},{13,12},{... | collective-permute-start | bytes 49160 | tf_op jit(solution)/shard_map/while/body/eval_jaxpr/ppermute | solution.py:18
  117.5 5.1 %collective-permute-start.1 = (f32[1,8,4,128]{3,2,1,0:T(4,128)S(1)}, f32[1,8,4,128]{3,2,1,0:T(4,128)S(1)}, u32[]{:S(2)}, u32[]{:S(2)}) collective-permute-start(f32[1,8,4,128]{3,2,1,0:T(4,128)S(1)} %pad_maximum_fusion.6), channel_id=1, source_target_pairs={{0,1},{1,2},{2,3},{4,5},{5,6},{6,7},{8,9},{9,10},{10,11},{12,13},{... | collective-permute-start | bytes 49160 | tf_op jit(solution)/shard_map/while/body/eval_jaxpr/ppermute | solution.py:15
  119.6 5.6 %collective-permute-start = (f32[1,8,4,128]{3,2,1,0:T(4,128)S(1)}, f32[1,8,4,128]{3,2,1,0:T(4,128)S(1)}, u32[]{:S(2)}, u32[]{:S(2)}) collective-permute-start(f32[1,8,4,128]{3,2,1,0:T(4,128)S(1)} %pad_maximum_fusion.6), channel_id=1, source_target_pairs={{1,0},{2,1},{3,2},{5,4},{6,5},{7,6},{9,8},{10,9},{11,10},{13,12},{... | collective-permute-start | bytes 49160 | tf_op jit(solution)/shard_map/while/body/eval_jaxpr/ppermute | solution.py:18
  131.3 5.1 %collective-permute-start.1 = (f32[1,8,4,128]{3,2,1,0:T(4,128)S(1)}, f32[1,8,4,128]{3,2,1,0:T(4,128)S(1)}, u32[]{:S(2)}, u32[]{:S(2)}) collective-permute-start(f32[1,8,4,128]{3,2,1,0:T(4,128)S(1)} %pad_maximum_fusion.6), channel_id=1, source_target_pairs={{0,1},{1,2},{2,3},{4,5},{5,6},{6,7},{8,9},{9,10},{10,11},{12,13},{... | collective-permute-start | bytes 49160 | tf_op jit(solution)/shard_map/while/body/eval_jaxpr/ppermute | solution.py:15
  133.4 5.6 %collective-permute-start = (f32[1,8,4,128]{3,2,1,0:T(4,128)S(1)}, f32[1,8,4,128]{3,2,1,0:T(4,128)S(1)}, u32[]{:S(2)}, u32[]{:S(2)}) collective-permute-start(f32[1,8,4,128]{3,2,1,0:T(4,128)S(1)} %pad_maximum_fusion.6), channel_id=1, source_target_pairs={{1,0},{2,1},{3,2},{5,4},{6,5},{7,6},{9,8},{10,9},{11,10},{13,12},{... | collective-permute-start | bytes 49160 | tf_op jit(solution)/shard_map/while/body/eval_jaxpr/ppermute | solution.py:18
  145.1 5.1 %collective-permute-start.1 = (f32[1,8,4,128]{3,2,1,0:T(4,128)S(1)}, f32[1,8,4,128]{3,2,1,0:T(4,128)S(1)}, u32[]{:S(2)}, u32[]{:S(2)}) collective-permute-start(f32[1,8,4,128]{3,2,1,0:T(4,128)S(1)} %pad_maximum_fusion.6), channel_id=1, source_target_pairs={{0,1},{1,2},{2,3},{4,5},{5,6},{6,7},{8,9},{9,10},{10,11},{12,13},{... | collective-permute-start | bytes 49160 | tf_op jit(solution)/shard_map/while/body/eval_jaxpr/ppermute | solution.py:15
  147.2 5.6 %collective-permute-start = (f32[1,8,4,128]{3,2,1,0:T(4,128)S(1)}, f32[1,8,4,128]{3,2,1,0:T(4,128)S(1)}, u32[]{:S(2)}, u32[]{:S(2)}) collective-permute-start(f32[1,8,4,128]{3,2,1,0:T(4,128)S(1)} %pad_maximum_fusion.6), channel_id=1, source_target_pairs={{1,0},{2,1},{3,2},{5,4},{6,5},{7,6},{9,8},{10,9},{11,10},{13,12},{... | collective-permute-start | bytes 49160 | tf_op jit(solution)/shard_map/while/body/eval_jaxpr/ppermute | solution.py:18
  158.9 5.1 %collective-permute-start.1 = (f32[1,8,4,128]{3,2,1,0:T(4,128)S(1)}, f32[1,8,4,128]{3,2,1,0:T(4,128)S(1)}, u32[]{:S(2)}, u32[]{:S(2)}) collective-permute-start(f32[1,8,4,128]{3,2,1,0:T(4,128)S(1)} %pad_maximum_fusion.6), channel_id=1, source_target_pairs={{0,1},{1,2},{2,3},{4,5},{5,6},{6,7},{8,9},{9,10},{10,11},{12,13},{... | collective-permute-start | bytes 49160 | tf_op jit(solution)/shard_map/while/body/eval_jaxpr/ppermute | solution.py:15
  160.9 5.6 %collective-permute-start = (f32[1,8,4,128]{3,2,1,0:T(4,128)S(1)}, f32[1,8,4,128]{3,2,1,0:T(4,128)S(1)}, u32[]{:S(2)}, u32[]{:S(2)}) collective-permute-start(f32[1,8,4,128]{3,2,1,0:T(4,128)S(1)} %pad_maximum_fusion.6), channel_id=1, source_target_pairs={{1,0},{2,1},{3,2},{5,4},{6,5},{7,6},{9,8},{10,9},{11,10},{13,12},{... | collective-permute-start | bytes 49160 | tf_op jit(solution)/shard_map/while/body/eval_jaxpr/ppermute | solution.py:18
  172.7 5.1 %collective-permute-start.1 = (f32[1,8,4,128]{3,2,1,0:T(4,128)S(1)}, f32[1,8,4,128]{3,2,1,0:T(4,128)S(1)}, u32[]{:S(2)}, u32[]{:S(2)}) collective-permute-start(f32[1,8,4,128]{3,2,1,0:T(4,128)S(1)} %pad_maximum_fusion.6), channel_id=1, source_target_pairs={{0,1},{1,2},{2,3},{4,5},{5,6},{6,7},{8,9},{9,10},{10,11},{12,13},{... | collective-permute-start | bytes 49160 | tf_op jit(solution)/shard_map/while/body/eval_jaxpr/ppermute | solution.py:15
  174.7 5.6 %collective-permute-start = (f32[1,8,4,128]{3,2,1,0:T(4,128)S(1)}, f32[1,8,4,128]{3,2,1,0:T(4,128)S(1)}, u32[]{:S(2)}, u32[]{:S(2)}) collective-permute-start(f32[1,8,4,128]{3,2,1,0:T(4,128)S(1)} %pad_maximum_fusion.6), channel_id=1, source_target_pairs={{1,0},{2,1},{3,2},{5,4},{6,5},{7,6},{9,8},{10,9},{11,10},{13,12},{... | collective-permute-start | bytes 49160 | tf_op jit(solution)/shard_map/while/body/eval_jaxpr/ppermute | solution.py:18
  186.2 1.7 copy-start
  191.2 4.9 %copy-start.2 = (f32[1,8,128,128]{3,2,1,0:T(8,128)S(1)}, f32[1,8,128,128]{3,2,1,0:T(8,128)}, u32[]{:S(2)}) copy-start(f32[1,8,128,128]{3,2,1,0:T(8,128)} %param.12) | copy-start | bytes 1572868
  191.2 66.1 %all-to-all-start = ((f32[8,1,8,64,128]{4,3,2,1,0:T(8,128)}), f32[8,1,8,64,128]{4,3,2,1,0:T(8,128)}, u32[]{:S(2)}, u32[]{:S(2)}) async-start(f32[8,1,8,64,128]{4,3,2,1,0:T(8,128)} %stack.9), calls=%async_computation | async-start | bytes 4194304 | tf_op jit(solution)/shard_map/all_to_all | solution.py:85
  196.1 61.2 %all-reduce.6.cloned.1.call-start = ((), (), s32[]{:S(2)}) async-start(), calls=%async_computation.1 | async-start | bytes 524288 | tf_op jit(solution)/shard_map/psum | solution.py:25
  306.4 12.3 %copy-start.4 = (f32[1,8,128,128]{3,2,1,0:T(8,128)}, f32[1,8,128,128]{3,2,1,0:T(8,128)S(1)}, u32[]{:S(2)}) copy-start(f32[1,8,128,128]{3,2,1,0:T(8,128)S(1)} %add.163) | copy-start | bytes 1572868
  306.4 11.4 %collective-permute-start.2 = (f32[8,128,128]{2,1,0:T(8,128)S(1)}, f32[8,128,128]{2,1,0:T(8,128)S(1)}, u32[]{:S(2)}, u32[]{:S(2)}) collective-permute-start(f32[8,128,128]{2,1,0:T(8,128)S(1)} %bitcast.114), channel_id=1, source_target_pairs={{0,4},{4,8},{8,12},{12,16},{16,20},{20,24},{24,28},{1,5},{5,9},{9,... | collective-permute-start | bytes 1572872 | tf_op jit(solution)/shard_map/ppermute | solution.py:31
Sparse Core Ops, SparseCore 0:
  200.5 56.7 all-reduce.5
